TPU v7x, 32 devices: a whole 2x2x4 slice. The times are simulated.
32 devices in a mesh: row: 8 (over y, x, core), col: 4 (over z).
Axes of the slice: x: 2, y: 2, z: 4, core: 2. Of those that a mesh axis runs over, the one named last changes fastest.
Arguments:
- out_grads: bfloat16 [64, 28672], P('col', 'row'), may hold values from -6 to 6
- in_acts: bfloat16 [64, 8192], P('row', 'col'), may hold values from -6 to 6
- out_basis: bfloat16 [28672, 28672], P('row', 'col'), may hold values from -0.03125 to 0.03125
- in_basis: bfloat16 [8192, 8192], P('col', 'row'), may hold values from -0.0625 to 0.0625
- eigenvalues: bfloat16 [28672, 8192], P('col', 'row'), may hold values from 0.019897461 to 2
- queries: bfloat16 [2, 28672, 8192], P(None, 'col', 'row'), may hold values from -0.00015640259 to 0.00015640259
Outputs:
- scores: float32 [2, 64], replicated
All inputs are finite; a program needn't handle non-finite values.
Results may differ from a plain program's by a relative error of at most 0.0045.
Values may be sent and summed in bfloat16 or wider, within the bound.
No kernel may reach another device: no remote copies, remote signals or barrier semaphores. Data moves between devices by JAX's collectives and lax.ppermute only.
A program may use at most 192 MiB of HBM per device.

v0:
```python
import jax
import jax.numpy as jnp
from jax import lax
from jax.sharding import PartitionSpec as P

DAMPING = 0.1


def local(out_grads, in_acts, out_basis, in_basis, eigenvalues, queries):
    grads_all = lax.all_gather(out_grads, "col", axis=0, tiled=True)
    grad_mine = lax.psum_scatter(
        jnp.dot(grads_all, out_basis, preferred_element_type=jnp.float32),
        "row",
        scatter_dimension=0,
        tiled=True,
    ).astype(jnp.bfloat16)
    grad_rot = lax.all_gather(grad_mine, "row", axis=0, tiled=True)
    acts_all = lax.all_gather(in_acts, "row", axis=0, tiled=True)
    act_part = jnp.dot(acts_all, in_basis, preferred_element_type=jnp.float32)
    act_rot = lax.psum(act_part, "col").astype(jnp.bfloat16)
    shifted = eigenvalues.astype(jnp.float32) + DAMPING
    scaled = queries.astype(jnp.float32) / shifted[None]
    lifted = jnp.einsum(
        "qkj,tj->qkt",
        scaled,
        act_rot.astype(jnp.float32),
        precision=lax.Precision.HIGHEST,
        preferred_element_type=jnp.float32,
    )
    partial_scores = jnp.einsum(
        "qkt,tk->qt", lifted, grad_rot.astype(jnp.float32), precision=lax.Precision.HIGHEST
    )
    return lax.psum(partial_scores, ("row", "col"))


def solution(mesh):
    in_specs = (
        P("col", "row"),
        P("row", "col"),
        P("row", "col"),
        P("col", "row"),
        P("col", "row"),
        P(None, "col", "row"),
    )
    out_specs = P()
    return jax.shard_map(local, mesh=mesh, in_specs=in_specs, out_specs=out_specs, check_vma=False)
```

profile of v0, /device:TPU:0, one launch (start us, length us, event | category | flops | bytes accessed | tf_op | source)
XLA Modules:
  0.0 220.7 jit_solution(7782558009660924071)
XLA Ops:
  6.5 0.0 reduce-scatter.2.cloned.1.call-start
  6.5 17.0 %all_gather.9 = bf16[64,3584]{1,0:T(8,128)(2,1)S(1)} all-gather(bf16[16,3584]{1,0:T(8,128)(2,1)} %param.6), channel_id=1, replica_groups=mesh['row'=8,'col'=4] {'col'}, dimensions={0}, use_global_device_ids=true | all-gather | bytes 573440 | tf_op jit(solution)/shard_map/all_gather | solution.py:10
  23.5 21.8 %fusion.7 = f32[64,7168]{1,0:T(8,128)} fusion(bf16[64,3584]{1,0:T(8,128)(2,1)S(1)} %all_gather.9, bf16[3584,7168]{1,0:T(8,128)(2,1)} %param.8), kind=kOutput, calls=%fused_computation.9 | convolution fusion | flops 3288334336 | bytes 53673984 | tf_op jit(solution)/shard_map/dot_general | solution.py:12
  45.3 0.0 copy-start.1
  45.3 0.0 reduce-scatter.2.cloned.1.call-update
  45.4 0.0 copy-start
  45.4 17.4 %convert_add_fusion = f32[7168,1024]{1,0:T(8,128)} fusion(bf16[7168,1024]{1,0:T(8,128)(2,1)} %param.10), kind=kLoop, calls=%fused_computation.3 | loop fusion | flops 14680064 | bytes 44040192 | tf_op jit(solution)/shard_map/add | solution.py:21
  62.8 0.0 copy-done.1
  62.8 9.4 %all_gather.11 = bf16[64,2048]{1,0:T(8,128)(2,1)S(1)} all-gather(bf16[8,2048]{1,0:T(8,128)(2,1)S(1)} %copy-done.1), channel_id=1, replica_groups=mesh['row'=8,'col'=4] {'row'}, dimensions={0}, use_global_device_ids=true | all-gather | bytes 294912 | tf_op jit(solution)/shard_map/all_gather | solution.py:18
  72.2 0.0 copy-done
  72.2 0.8 fusion.8
  73.1 25.6 %all-reduce.1 = bf16[64,1024]{1,0:T(8,128)(2,1)S(1)} all-reduce(f32[64,1024]{1,0:T(8,128)S(1)} %fusion.8), channel_id=1, replica_groups=mesh['row'=8,'col'=4] {'col'}, use_global_device_ids=true, to_apply=%region_1.0 | all-reduce | flops 65536 | bytes 393216 | tf_op jit(solution)/shard_map/psum | solution.py:20
  98.7 45.4 %fusion = f32[2,7168,64]{1,2,0:T(8,128)} fusion(bf16[2,7168,1024]{2,1,0:T(8,128)(2,1)} %param.11, f32[7168,1024]{1,0:T(8,128)} %convert_add_fusion, bf16[64,1024]{1,0:T(8,128)(2,1)S(1)} %all-reduce.1), kind=kOutput, calls=%fused_computation.1 | convolution fusion | flops 11303649280 | bytes 62521344 | tf_op jit(solution)/shard_map/qkj,tj->qkt/dot_general | solution.py:23
  144.1 0.0 reduce-scatter.2.cloned.1.call-done
  144.1 1.0 convert_element_type.14
  145.1 11.0 %all_gather.10 = bf16[64,7168]{1,0:T(8,128)(2,1)S(1)} all-gather(bf16[8,7168]{1,0:T(8,128)(2,1)S(1)} %convert_element_type.14), channel_id=1, replica_groups=mesh['row'=8,'col'=4] {'row'}, dimensions={0}, use_global_device_ids=true | all-gather | bytes 1032192 | tf_op jit(solution)/shard_map/all_gather | solution.py:17
  156.0 19.9 %fusion.2 = f32[64,1,2]{2,1,0:T(1,128)S(1)} fusion(f32[2,7168,64]{1,2,0:T(8,128)} %fusion, bf16[64,7168,1]{1,0,2:T(8,128)(2,1)S(1)} %bitcast.11), kind=kOutput, calls=%fused_computation.4 | convolution fusion | flops 11010048 | bytes 4588032 | tf_op jit(solution)/shard_map/qkt,tk->qt/dot_general | solution.py:30
  175.9 0.1 copy.9
  176.0 37.8 %psum.15 = f32[2,64]{1,0:T(2,128)} all-reduce(f32[2,64]{1,0:T(2,128)S(1)} %bitcast.12), channel_id=1, replica_groups=mesh['row'=8,'col'=4] {'row','col'}, use_global_device_ids=true, to_apply=%region_2.0 | all-reduce | flops 128 | bytes 1024 | tf_op jit(solution)/shard_map/psum | solution.py:33
Async XLA Ops:
  6.5 137.6 %reduce-scatter.2.cloned.1.call-start = ((), (), s32[]{:S(2)}) async-start(), calls=%async_computation.1 | async-start | bytes 2064384 | tf_op jit(solution)/shard_map/reduce_scatter | solution.py:11
  45.3 17.4 %copy-start.1 = (bf16[8,2048]{1,0:T(8,128)(2,1)S(1)}, bf16[8,2048]{1,0:T(8,128)(2,1)}, u32[]{:S(2)}) copy-start(bf16[8,2048]{1,0:T(8,128)(2,1)} %param.7) | copy-start | bytes 98308
  45.4 26.8 %copy-start = (bf16[2048,1024]{1,0:T(8,128)(2,1)S(1)}, bf16[2048,1024]{1,0:T(8,128)(2,1)}, u32[]{:S(2)}) copy-start(bf16[2048,1024]{1,0:T(8,128)(2,1)} %param.9) | copy-start | bytes 12582916
Sparse Core Ops, SparseCore 0:
  45.5 42.0 reduce-scatter.1
where the time goes:
time: 221 us
  blocking collectives  101 us (46%)
  matrix products  88 us (40%)
  other arithmetic  18.3 us (8%)
  between operations  13.4 us (6%)
    dot_general x1, matrix products, local(): jnp.einsum('qkj,tj->qkt', scaled, act_rot.astype(jnp.float32), precision=...  45.4 us
    psum x1, blocking collectives, local(): return lax.psum(partial_scores, ('row', 'col'))  37.8 us
    psum x1, blocking collectives, local(): act_rot = lax.psum(act_part, 'col').astype(jnp.bfloat16)  25.6 us
    dot_general x1, matrix products, local(): jnp.dot(grads_all, out_basis, preferred_element_type=jnp.float32)  21.8 us
    dot_general x1, matrix products, local(): jnp.einsum('qkt,tk->qt', lifted, grad_rot.astype(jnp.float32), precision=...  19.9 us
    add x1, other arithmetic, local(): shifted = eigenvalues.astype(jnp.float32) + DAMPING  17.4 us
    all_gather x1, blocking collectives, local(): grads_all = lax.all_gather(out_grads, 'col', axis=0, tiled=True)  17 us
    all_gather x1, blocking collectives, local(): grad_rot = lax.all_gather(grad_mine, 'row', axis=0, tiled=True)  11 us
  transfers between devices with their start and end apart: 1, of which 0 were waited for; matrix products, arithmetic and copies ran while one was open for 29% of the time, Pallas kernels for 0%

commit v1 on v0

--- a/solution.py
+++ b/solution.py
@@ -7,7 +7,16 @@
 
 
 def local(out_grads, in_acts, out_basis, in_basis, eigenvalues, queries):
-    grads_all = lax.all_gather(out_grads, "col", axis=0, tiled=True)
+    ways = lax.axis_size("col")
+    up = [(d, (d + 1) % ways) for d in range(ways)]
+    down = [(d, (d - 1) % ways) for d in range(ways)]
+    earlier, later = ([out_grads], [out_grads])
+    for _ in range(ways // 2):
+        earlier.append(lax.ppermute(earlier[-1], "col", up))
+    for _ in range((ways - 1) // 2):
+        later.append(lax.ppermute(later[-1], "col", down))
+    line = jnp.concatenate([*earlier[::-1], *later[1:]], axis=0)
+    grads_all = jnp.roll(line, (lax.axis_index("col") - ways // 2) * out_grads.shape[0], axis=0)
     grad_mine = lax.psum_scatter(
         jnp.dot(grads_all, out_basis, preferred_element_type=jnp.float32),
         "row",

time: 221 us -> 208 us (0.941)
  blocking collectives: 101 us -> 83.4 us
  starting transfers between devices: 0.01 us -> 5.22 us
    all_gather x1 -> x0, blocking collectives: 17 us -> none  [local(): grads_all = lax.all_gather(out_grads, 'col', axis=0, tiled=True)]
    ppermute x0 -> x3, starting transfers between devices: none -> 5.22 us  [the longest x2 3.13 us: local(): earlier.append(lax.ppermute(earlier[-1], 'col', up))]
  transfers between devices with their start and end apart: 1 -> 4, of which waited for: 0 -> 0; matrix products, arithmetic and copies ran while one was open for 29% -> 30% of each run, Pallas kernels for 0% -> 0%
where the time goes in v1:
time: 208 us
  matrix products  88 us (42%)
  blocking collectives  83.4 us (40%)
  other arithmetic  17.6 us (8%)
  between operations  13.5 us (6%)
  starting transfers between devices  5.22 us (3%)
    dot_general x1, matrix products, local(): jnp.einsum('qkj,tj->qkt', scaled, act_rot.astype(jnp.float32), precision=...  45.4 us
    psum x1, blocking collectives, local(): return lax.psum(partial_scores, ('row', 'col'))  37.8 us
    psum x1, blocking collectives, local(): act_rot = lax.psum(act_part, 'col').astype(jnp.bfloat16)  25.3 us
    dot_general x1, matrix products, local(): jnp.dot(grads_all, out_basis, preferred_element_type=jnp.float32)  21.8 us
    dot_general x1, matrix products, local(): jnp.einsum('qkt,tk->qt', lifted, grad_rot.astype(jnp.float32), precision=...  19.9 us
    add x1, other arithmetic, local(): shifted = eigenvalues.astype(jnp.float32) + DAMPING  16.7 us
    all_gather x1, blocking collectives, local(): grad_rot = lax.all_gather(grad_mine, 'row', axis=0, tiled=True)  10.8 us
    all_gather x1, blocking collectives, local(): acts_all = lax.all_gather(in_acts, 'row', axis=0, tiled=True)  9.46 us
  transfers between devices with their start and end apart: 4, of which 0 were waited for; matrix products, arithmetic and copies ran while one was open for 30% of the time, Pallas kernels for 0%

profile of v1, /device:TPU:0, one launch (start us, length us, event | category | flops | bytes accessed | tf_op | source)
XLA Modules:
  0.0 208.0 jit_solution(16248548653670170509)
XLA Ops:
  6.5 0.0 copy-start.1
  6.5 0.0 copy-start.2
  6.5 0.0 reduce-scatter.2.cloned.1.call-start
  6.5 0.0 copy-start
  6.5 3.1 %collective-permute-start = (bf16[16,3584]{1,0:T(8,128)(2,1)}, bf16[16,3584]{1,0:T(8,128)(2,1)S(1)}, u32[]{:S(2)}, u32[]{:S(2)}) collective-permute-start(bf16[16,3584]{1,0:T(8,128)(2,1)} %param.6), channel_id=1, source_target_pairs={{0,1},{1,2},{2,3},{3,0},{4,5},{5,6},{6,7},{7,4},{8,9},{9,10},{10,1... | collective-permute-start | bytes 344072 | tf_op jit(solution)/shard_map/ppermute | solution.py:15
  9.6 2.1 %collective-permute-start.2 = (bf16[16,3584]{1,0:T(8,128)(2,1)}, bf16[16,3584]{1,0:T(8,128)(2,1)S(1)}, u32[]{:S(2)}, u32[]{:S(2)}) collective-permute-start(bf16[16,3584]{1,0:T(8,128)(2,1)} %param.6), channel_id=1, source_target_pairs={{0,3},{1,0},{2,1},{3,2},{4,7},{5,4},{6,5},{7,6},{8,11},{9,8},{10,9... | collective-permute-start | bytes 344072 | tf_op jit(solution)/shard_map/ppermute | solution.py:17
  11.7 16.7 %convert_add_fusion = f32[7168,1024]{1,0:T(8,128)} fusion(bf16[7168,1024]{1,0:T(8,128)(2,1)} %param.10), kind=kLoop, calls=%fused_computation.3 | loop fusion | flops 14680064 | bytes 44040192 | tf_op jit(solution)/shard_map/add | solution.py:30
  28.4 0.0 copy-done.2
  28.4 9.5 %all_gather.7 = bf16[64,2048]{1,0:T(8,128)(2,1)S(1)} all-gather(bf16[8,2048]{1,0:T(8,128)(2,1)S(1)} %copy-done.2), channel_id=1, replica_groups=mesh['row'=8,'col'=4] {'row'}, dimensions={0}, use_global_device_ids=true | all-gather | bytes 294912 | tf_op jit(solution)/shard_map/all_gather | solution.py:27
  37.8 0.0 copy-done
  37.8 0.8 fusion.10
  38.7 0.0 collective-permute-done
  38.7 0.1 collective-permute-start.1
  38.8 25.3 %all-reduce.1 = bf16[64,1024]{1,0:T(8,128)(2,1)S(1)} all-reduce(f32[64,1024]{1,0:T(8,128)S(1)} %fusion.10), channel_id=1, replica_groups=mesh['row'=8,'col'=4] {'col'}, use_global_device_ids=true, to_apply=%region_1.2 | all-reduce | flops 65536 | bytes 393216 | tf_op jit(solution)/shard_map/psum | solution.py:29
  64.2 0.0 collective-permute-done.1
  64.2 0.0 copy-done.1
  64.2 0.0 collective-permute-done.2
  64.3 21.8 %fusion.5 = f32[64,7168]{1,0:T(8,128)} fusion(bf16[3584,7168]{1,0:T(8,128)(2,1)} %param.8, bf16[128,3584]{1,0:T(8,128)(2,1)S(1)} %constant_dynamic-update-slice_fusion, s32[]{:T(128)S(6)} %select_n.14), kind=kOutput, calls=%fused_computation.7 | convolution fusion | flops 3288334336 | bytes 53673988 | tf_op jit(solution)/shard_map/dot_general | solution.py:21
  86.2 0.0 reduce-scatter.2.cloned.1.call-update
  86.2 45.4 %fusion = f32[2,7168,64]{1,2,0:T(8,128)} fusion(bf16[2,7168,1024]{2,1,0:T(8,128)(2,1)} %param.11, f32[7168,1024]{1,0:T(8,128)} %convert_add_fusion, bf16[64,1024]{1,0:T(8,128)(2,1)S(1)} %all-reduce.1), kind=kOutput, calls=%fused_computation.1 | convolution fusion | flops 11303649280 | bytes 62521344 | tf_op jit(solution)/shard_map/qkj,tj->qkt/dot_general | solution.py:32
  131.6 0.0 reduce-scatter.2.cloned.1.call-done
  131.6 1.0 convert_element_type.14
  132.5 10.8 %all_gather.6 = bf16[64,7168]{1,0:T(8,128)(2,1)S(1)} all-gather(bf16[8,7168]{1,0:T(8,128)(2,1)S(1)} %convert_element_type.14), channel_id=1, replica_groups=mesh['row'=8,'col'=4] {'row'}, dimensions={0}, use_global_device_ids=true | all-gather | bytes 1032192 | tf_op jit(solution)/shard_map/all_gather | solution.py:26
  143.4 19.9 %fusion.2 = f32[64,1,2]{2,1,0:T(1,128)S(1)} fusion(f32[2,7168,64]{1,2,0:T(8,128)} %fusion, bf16[64,7168,1]{1,0,2:T(8,128)(2,1)S(1)} %bitcast.10), kind=kOutput, calls=%fused_computation.4 | convolution fusion | flops 11010048 | bytes 4588032 | tf_op jit(solution)/shard_map/qkt,tk->qt/dot_general | solution.py:39
  163.3 0.1 copy.9
  163.4 37.8 %psum.15 = f32[2,64]{1,0:T(2,128)} all-reduce(f32[2,64]{1,0:T(2,128)S(1)} %bitcast.11), channel_id=1, replica_groups=mesh['row'=8,'col'=4] {'row','col'}, use_global_device_ids=true, to_apply=%region_2.3 | all-reduce | flops 128 | bytes 1024 | tf_op jit(solution)/shard_map/psum | solution.py:42
  (8 shorter events, 0.1 us)
Async XLA Ops:
  6.5 57.7 %copy-start.1 = (bf16[16,3584]{1,0:T(8,128)(2,1)S(1)}, bf16[16,3584]{1,0:T(8,128)(2,1)}, u32[]{:S(2)}) copy-start(bf16[16,3584]{1,0:T(8,128)(2,1)} %param.6) | copy-start | bytes 344068
  6.5 21.8 %copy-start.2 = (bf16[8,2048]{1,0:T(8,128)(2,1)S(1)}, bf16[8,2048]{1,0:T(8,128)(2,1)}, u32[]{:S(2)}) copy-start(bf16[8,2048]{1,0:T(8,128)(2,1)} %param.7) | copy-start | bytes 98308
  6.5 125.0 %reduce-scatter.2.cloned.1.call-start = ((), (), s32[]{:S(2)}) async-start(), calls=%async_computation.1 | async-start | bytes 2064384 | tf_op jit(solution)/shard_map/reduce_scatter | solution.py:20
  6.5 31.3 %copy-start = (bf16[2048,1024]{1,0:T(8,128)(2,1)S(1)}, bf16[2048,1024]{1,0:T(8,128)(2,1)}, u32[]{:S(2)}) copy-start(bf16[2048,1024]{1,0:T(8,128)(2,1)} %param.9) | copy-start | bytes 12582916
  6.5 32.2 %collective-permute-start = (bf16[16,3584]{1,0:T(8,128)(2,1)}, bf16[16,3584]{1,0:T(8,128)(2,1)S(1)}, u32[]{:S(2)}, u32[]{:S(2)}) collective-permute-start(bf16[16,3584]{1,0:T(8,128)(2,1)} %param.6), channel_id=1, source_target_pairs={{0,1},{1,2},{2,3},{3,0},{4,5},{5,6},{6,7},{7,4},{8,9},{9,10},{10,1... | collective-permute-start | bytes 344072 | tf_op jit(solution)/shard_map/ppermute | solution.py:15
  9.6 54.6 %collective-permute-start.2 = (bf16[16,3584]{1,0:T(8,128)(2,1)}, bf16[16,3584]{1,0:T(8,128)(2,1)S(1)}, u32[]{:S(2)}, u32[]{:S(2)}) collective-permute-start(bf16[16,3584]{1,0:T(8,128)(2,1)} %param.6), channel_id=1, source_target_pairs={{0,3},{1,0},{2,1},{3,2},{4,7},{5,4},{6,5},{7,6},{8,11},{9,8},{10,9... | collective-permute-start | bytes 344072 | tf_op jit(solution)/shard_map/ppermute | solution.py:17
  38.7 25.5 %collective-permute-start.1 = (bf16[16,3584]{1,0:T(8,128)(2,1)S(1)}, bf16[16,3584]{1,0:T(8,128)(2,1)S(1)}, u32[]{:S(2)}, u32[]{:S(2)}) collective-permute-start(bf16[16,3584]{1,0:T(8,128)(2,1)S(1)} %collective-permute-done), channel_id=1, source_target_pairs={{0,1},{1,2},{2,3},{3,0},{4,5},{5,6},{6,7},{7,4},{8,9},{9,10},{10,1... | collective-permute-start | bytes 344072 | tf_op jit(solution)/shard_map/ppermute | solution.py:15
Sparse Core Ops, SparseCore 0:
  86.3 37.2 reduce-scatter.1
